TPU v7x, 512 devices: a whole 4x8x8 slice. The times are simulated.
512 devices in a mesh: seq: 64 (over y, x, core), fsdp: 8 (over z).
Axes of the slice: x: 4, y: 8, z: 8, core: 2. Of those that a mesh axis runs over, the one named last changes fastest.
Arguments:
- queries: bfloat16 [32768, 2048], P('seq', 'fsdp'), may hold values from -6 to 6
- keys: bfloat16 [32768, 2048], P('seq', 'fsdp'), may hold values from -6 to 6
- values: bfloat16 [32768, 2048], P('seq', 'fsdp'), may hold values from -6 to 6
- feature_weight: bfloat16 [16, 128, 128], P(None, 'fsdp', 'seq'), may hold values from -0.5 to 0.5
- norm_gain: bfloat16 [16, 128], P('fsdp'), may hold values from 0.099609375 to 1.8984375
- doc_bounds: int32 [4, 2], replicated, may hold values from 0 to 256, as said below
- out_grad: bfloat16 [32768, 2048], P('seq', 'fsdp'), may hold values from -6 to 6
Outputs:
- mixed: bfloat16 [32768, 2048], P('seq', 'fsdp')
- query_grad: bfloat16 [32768, 2048], P('seq', 'fsdp')
- key_grad: bfloat16 [32768, 2048], P('seq', 'fsdp')
- value_grad: bfloat16 [32768, 2048], P('seq', 'fsdp')
- weight_grad: float32 [16, 128, 128], P(None, 'fsdp', 'seq')
- gain_grad: float32 [16, 128], P('fsdp')
Inputs may be any that keep to these rules, and one draw needn't show every extreme that they name: `doc_bounds`: the rows list the 4 documents in order: column 0 is the first block and column 1 the block after the last; the first document starts at block 0, each ends where the next starts, the last ends at block 256; every document holds one block or more of 128 tokens.
All inputs are finite; a program needn't handle non-finite values.
Results may differ from a plain program's by a relative error of at most 0.015.
Values may be sent and summed in bfloat16 or wider, within the bound.
No kernel may reach another device: no remote copies, remote signals or barrier semaphores. Data moves between devices by JAX's collectives and lax.ppermute only.
A program may use at most 64 MiB of HBM per device.

v0:
```python
import jax
import jax.numpy as jnp
from jax import lax
from jax.sharding import PartitionSpec as P

HS = 128
BLK = 128
epsilon = 1.0


def carried_in(shard, axis, join, neutral, backward):
    count = lax.axis_size(axis)
    place = lax.axis_index(axis)
    ahead = count - 1 - place if backward else place
    gathered = jax.tree.map(
        lambda a, kind: lax.all_gather(a.astype(kind), axis), shard, (jnp.bfloat16, jnp.bfloat16)
    )
    state = jax.tree.map(lambda a, e: jnp.zeros_like(a) + jnp.asarray(e, a.dtype), shard, neutral)

    def one(hop, state):
        source = count - 1 - hop if backward else hop
        return join(
            state,
            jax.tree.map(
                lambda a, own: lax.dynamic_index_in_dim(a, source, 0, False).astype(own.dtype),
                gathered,
                shard,
            ),
        )

    return lax.fori_loop(0, ahead, one, state)


def chain_states(earlier, later):
    early_state, early_flag = earlier
    late_state, late_flag = later
    return (
        jnp.where(late_flag > 0.0, late_state, early_state + late_state),
        jnp.maximum(early_flag, late_flag),
    )


def project(rows, weight):
    return jnp.einsum("bthd,hde->bthe", rows, weight, preferred_element_type=jnp.float32).astype(
        jnp.bfloat16
    )


def local(queries, keys, values, feature_weight, norm_gain, doc_bounds, out_grad):
    rows_full = lax.all_gather(feature_weight, "seq", axis=2, tiled=True)
    weight_local = lax.all_to_all(rows_full, "fsdp", split_axis=0, concat_axis=1, tiled=True)
    head_count = weight_local.shape[0]
    tokens_here = queries.shape[0]
    block_count = tokens_here // BLK
    block_shape = (block_count, BLK, head_count, HS)
    query_blocks = queries.reshape(block_shape)
    key_blocks = keys.reshape(block_shape)
    value_blocks = values.reshape(block_shape)
    qfeat = project(query_blocks, weight_local)
    kfeat = project(key_blocks, weight_local)
    first_block = lax.axis_index("seq") * block_count
    block_ids = first_block + jnp.arange(block_count, dtype=jnp.int32)
    starts = doc_bounds[:, 0]
    starts_here = jnp.any(starts[None, :] == block_ids[:, None], axis=1)
    opened = jnp.cumsum(starts_here.astype(jnp.int32))
    reach_left = opened == 0
    reach_right = opened[-1] - opened == 0
    has_start = jnp.any(starts_here).astype(jnp.float32)
    updates = jnp.einsum("bthe,bthf->bhef", kfeat, value_blocks, preferred_element_type=jnp.float32)
    zero_state = jnp.zeros(updates.shape[1:], jnp.float32)
    zero_flag = jnp.zeros((), jnp.float32)
    running = zero_state
    prefix_list = []
    for position in range(block_count):
        held = jnp.where(starts_here[position], zero_state, running)
        prefix_list.append(held)
        running = held + updates[position]
    entering, _ = carried_in(
        (running, has_start), "seq", chain_states, (zero_state, zero_flag), False
    )
    states = jnp.stack(prefix_list) + jnp.where(
        reach_left[:, None, None, None], entering[None], 0.0
    )
    state_half = states.astype(jnp.bfloat16)
    causal = jnp.arange(BLK)[:, None] >= jnp.arange(BLK)[None, :]
    scores = jnp.einsum("bthe,bshe->bhts", qfeat, kfeat, preferred_element_type=jnp.float32)
    prob_half = jnp.where(causal, scores, 0.0).astype(jnp.bfloat16)
    mixed_f = jnp.einsum("bthe,bhef->bthf", qfeat, state_half, preferred_element_type=jnp.float32)
    mixed_f = mixed_f + jnp.einsum(
        "bhts,bshf->bthf", prob_half, value_blocks, preferred_element_type=jnp.float32
    )
    gains = norm_gain.astype(jnp.float32)
    inverse = lax.rsqrt(jnp.mean(mixed_f * mixed_f, axis=-1, keepdims=True) + epsilon)
    mixed = (mixed_f * inverse * gains).astype(jnp.bfloat16)
    grad_y = out_grad.reshape(block_shape).astype(jnp.float32)
    scaled = grad_y * gains
    grad_mix = inverse * (
        scaled - mixed_f * inverse * inverse * jnp.mean(scaled * mixed_f, axis=-1, keepdims=True)
    )
    grad_half = grad_mix.astype(jnp.bfloat16)
    gain_part = jnp.sum(grad_y * mixed_f * inverse, axis=(0, 1))
    state_grads = jnp.einsum(
        "bthe,bthf->bhef", qfeat, grad_half, preferred_element_type=jnp.float32
    )
    running = zero_state
    suffix_list = [zero_state] * block_count
    for position in reversed(range(block_count)):
        suffix_list[position] = running
        running = jnp.where(starts_here[position], zero_state, running + state_grads[position])
    leaving, _ = carried_in(
        (running, has_start), "seq", chain_states, (zero_state, zero_flag), True
    )
    suffix = jnp.stack(suffix_list) + jnp.where(
        reach_right[:, None, None, None], leaving[None], 0.0
    )
    suffix_half = suffix.astype(jnp.bfloat16)
    dot_grads = jnp.einsum(
        "bthf,bshf->bhts", grad_half, value_blocks, preferred_element_type=jnp.float32
    )
    dot_half = jnp.where(causal, dot_grads, 0.0).astype(jnp.bfloat16)
    qfeat_grad = jnp.einsum(
        "bthf,bhef->bthe", grad_half, state_half, preferred_element_type=jnp.float32
    )
    qfeat_grad = (
        qfeat_grad
        + jnp.einsum("bhts,bshe->bthe", dot_half, kfeat, preferred_element_type=jnp.float32)
    ).astype(jnp.bfloat16)
    kfeat_grad = jnp.einsum(
        "bshf,bhef->bshe", value_blocks, suffix_half, preferred_element_type=jnp.float32
    )
    kfeat_grad = (
        kfeat_grad
        + jnp.einsum("bhts,bthe->bshe", dot_half, qfeat, preferred_element_type=jnp.float32)
    ).astype(jnp.bfloat16)
    value_grad = jnp.einsum(
        "bshe,bhef->bshf", kfeat, suffix_half, preferred_element_type=jnp.float32
    )
    value_grad = (
        value_grad
        + jnp.einsum("bhts,bthf->bshf", prob_half, grad_half, preferred_element_type=jnp.float32)
    ).astype(jnp.bfloat16)
    query_grad = jnp.einsum(
        "bthe,hde->bthd", qfeat_grad, weight_local, preferred_element_type=jnp.float32
    ).astype(jnp.bfloat16)
    key_grad = jnp.einsum(
        "bthe,hde->bthd", kfeat_grad, weight_local, preferred_element_type=jnp.float32
    ).astype(jnp.bfloat16)
    weight_part = jnp.einsum(
        "bthd,bthe->hde", query_blocks, qfeat_grad, preferred_element_type=jnp.float32
    )
    weight_part = weight_part + jnp.einsum(
        "bthd,bthe->hde", key_blocks, kfeat_grad, preferred_element_type=jnp.float32
    )
    weight_sum, gain_sum = lax.psum((weight_part, gain_part), "seq")
    column_width = weight_sum.shape[2] // lax.axis_size("seq")
    weight_columns = lax.dynamic_slice_in_dim(
        weight_sum, lax.axis_index("seq") * column_width, column_width, 2
    )
    owned_grad = lax.all_to_all(weight_columns, "fsdp", split_axis=1, concat_axis=0, tiled=True)
    factor = (lax.axis_size("seq") * tokens_here) ** (-0.5)
    flat_shape = (tokens_here, head_count * HS)
    return (
        mixed.reshape(flat_shape),
        query_grad.reshape(flat_shape),
        key_grad.reshape(flat_shape),
        value_grad.reshape(flat_shape),
        owned_grad * factor,
        gain_sum * factor,
    )


def solution(mesh):
    placed = (
        P("seq", "fsdp"),
        P("seq", "fsdp"),
        P("seq", "fsdp"),
        P(None, "fsdp", "seq"),
        P("fsdp", None),
        P(),
        P("seq", "fsdp"),
    )
    return jax.shard_map(
        local,
        mesh=mesh,
        in_specs=placed,
        out_specs=(
            P("seq", "fsdp"),
            P("seq", "fsdp"),
            P("seq", "fsdp"),
            P("seq", "fsdp"),
            P(None, "fsdp", "seq"),
            P("fsdp", None),
        ),
        check_vma=False,
    )
```

profile of v0, /device:TPU:1, one launch (start us, length us, event | category | flops | bytes accessed | tf_op | source)
XLA Modules:
  0.0 827.8 jit_solution(3233053818263169173)
XLA Ops:
  8.0 53.9 %all_gather.19 = bf16[16,16,128]{1,0,2:T(8,128)(2,1)S(1)} all-gather(bf16[16,16,2]{1,0,2:T(8,128)(2,1)S(1)} %copy.146), channel_id=1, replica_groups=mesh['seq'=64,'fsdp'=8] {'seq'}, dimensions={2}, use_global_device_ids=true | all-gather | bytes 66560 | tf_op jit(solution)/shard_map/all_gather | solution.py:50
  61.8 1.1 copy.147
  62.9 8.9 %all-to-all-start = ((bf16[16,16,128]{2,1,0:T(8,128)(2,1)}), bf16[16,16,128]{2,1,0:T(8,128)(2,1)S(1)}, u32[]{:S(2)}, u32[]{:S(2)}) async-start(bf16[16,16,128]{2,1,0:T(8,128)(2,1)} %copy.147), calls=%async_computation | async-start | bytes 131072 | tf_op jit(solution)/shard_map/all_to_all | solution.py:51
  73.3 1.0 reshape.100
  74.3 1.0 reshape.101
  76.0 3.0 all-to-all-done
  79.5 2.5 fusion.43
  84.1 1.3 dynamic-slice
  86.1 125.5 %all-reduce = bf16[64]{0:T(256)(128)(2,1)S(1)} all-reduce(bf16[64]{0:T(256)(128)(2,1)S(1)} %dynamic-update-slice), channel_id=1, replica_groups=mesh['seq'=64,'fsdp'=8] {'seq'}, use_global_device_ids=true, to_apply=%add | all-reduce | flops 64 | bytes 256
  213.9 2.1 while.26
  215.1 0.9 add_select_fusion.4
  217.2 3.2 fusion.40
  220.8 1.2 fusion.48
  222.9 0.9 copy.160
  223.8 252.4 %psum.15 = f32[2,128]{1,0:T(2,128)S(1)} all-reduce(f32[2,128]{1,0:T(2,128)S(1)} %get-tuple-element.136), channel_id=1, replica_groups=mesh['seq'=64,'fsdp'=8] {'seq'}, use_global_device_ids=true, to_apply=%region_11.12 | all-reduce | flops 256 | bytes 2048 | tf_op jit(solution)/shard_map/psum | solution.py:154
  476.8 1.5 fusion.41
  478.3 1.9 copy_bitcast_fusion.2
  480.2 132.8 %while.27 = (s32[]{:T(128)}, f32[2,128,128]{2,1,0:T(8,128)S(1)}, s32[]{:T(128)}, bf16[64]{0:T(256)(128)(2,1)S(1)}, bf16[64,2,128,128]{3,2,1,0:T(8,128)(2,1)}, /*...) while((s32[]{:T(128)}, f32[2,128,128]{2,1,0:T(8,128)S(1)}, s32[]{:T(128)}, ...), condition=%wide.region_8.9_spmd, body=%wide.region_7.8_spmd.sunk | while | flops 98311 | bytes 327847 | solution.py:31
  613.0 1.4 fusion.29
  614.4 1.4 fusion.34
  616.2 0.9 fusion.14
  618.1 184.5 %all-reduce.3.cloned.1.call-done = f32[2,128,128]{1,2,0:T(8,128)} async-done(((f32[2,128,128]{1,2,0:T(8,128)}), f32[2,128,128]{1,2,0:T(8,128)}) %all-reduce.3.cloned.1.call-update) | async-done | bytes 131088 | tf_op jit(solution)/shard_map/psum | solution.py:154
  804.0 7.1 all-to-all-start.1
  812.0 8.5 %all-to-all-done.1 = f32[2,128,2]{2,0,1:T(2,128)S(1)} async-done(((f32[2,128,2]{2,0,1:T(2,128)}), f32[2,128,2]{2,0,1:T(2,128)S(1)}, u32[]{:S(2)}, u32[]{:S(2)}) %all-to-all-start.1) | async-done | bytes 2080 | tf_op jit(solution)/shard_map/all_to_all | solution.py:159
  (197 shorter events, 106.0 us)
Async XLA Ops:
  7.2 75.6 %copy-start.2 = (bf16[512,256]{1,0:T(8,128)(2,1)S(1)}, bf16[512,256]{1,0:T(8,128)(2,1)}, u32[]{:S(2)}) copy-start(bf16[512,256]{1,0:T(8,128)(2,1)} %param.11) | copy-start | bytes 786436
  7.2 76.4 %copy-start.1 = (bf16[512,256]{1,0:T(8,128)(2,1)S(1)}, bf16[512,256]{1,0:T(8,128)(2,1)}, u32[]{:S(2)}) copy-start(bf16[512,256]{1,0:T(8,128)(2,1)} %param.17) | copy-start | bytes 786436
  7.2 76.9 %copy-start.7 = (bf16[2,128]{1,0:T(2,128)(2,1)S(1)}, bf16[2,128]{1,0:T(2,128)(2,1)}, u32[]{:S(2)}) copy-start(bf16[2,128]{1,0:T(2,128)(2,1)} %param.15) | copy-start | bytes 1540
  62.9 16.1 %all-to-all-start = ((bf16[16,16,128]{2,1,0:T(8,128)(2,1)}), bf16[16,16,128]{2,1,0:T(8,128)(2,1)S(1)}, u32[]{:S(2)}, u32[]{:S(2)}) async-start(bf16[16,16,128]{2,1,0:T(8,128)(2,1)} %copy.147), calls=%async_computation | async-start | bytes 131072 | tf_op jit(solution)/shard_map/all_to_all | solution.py:51
  71.8 142.0 %all-gather.3.cloned.1.call-start = ((), (), s32[]{:S(2)}) async-start(), calls=%async_computation.2 | async-start | bytes 4259840 | tf_op jit(solution)/shard_map/all_gather | solution.py:16
  82.0 398.1 %all-gather.5.cloned.1.call-start = ((), (), s32[]{:S(2)}) async-start(), calls=%async_computation.3 | async-start | bytes 4259840 | tf_op jit(solution)/shard_map/all_gather | solution.py:16
  83.8 132.2 %copy-start.6 = (f32[1,2,128,128]{3,2,1,0:T(8,128)S(1)}, f32[1,2,128,128]{3,2,1,0:T(8,128)}, u32[]{:S(2)}) copy-start(f32[1,2,128,128]{3,2,1,0:T(8,128)} %get-tuple-element.165) | copy-start | bytes 393220
  212.9 3.7 copy-start.4
  216.0 6.3 copy-start.3
  220.4 582.1 %all-reduce.3.cloned.1.call-start = ((), (), s32[]{:S(2)}) async-start(), calls=%async_computation.4 | async-start | bytes 262144 | tf_op jit(solution)/shard_map/psum | solution.py:154
  223.8 390.6 %copy-start = (f32[1,2,128,128]{3,2,1,0:T(8,128)S(1)}, f32[1,2,128,128]{3,2,1,0:T(8,128)}, u32[]{:S(2)}) copy-start(f32[1,2,128,128]{3,2,1,0:T(8,128)} %get-tuple-element.161) | copy-start | bytes 393220
  478.3 134.7 %copy-start.5 = (f32[1,2,128,128]{3,2,1,0:T(8,128)}, f32[1,2,128,128]{3,2,1,0:T(8,128)S(1)}, u32[]{:S(2)}) copy-start(f32[1,2,128,128]{3,2,1,0:T(8,128)S(1)} %fusion.41) | copy-start | bytes 393220
  804.0 16.4 %all-to-all-start.1 = ((f32[2,128,2]{2,0,1:T(2,128)}), f32[2,128,2]{2,0,1:T(2,128)S(1)}, u32[]{:S(2)}, u32[]{:S(2)}) async-start(f32[2,128,2]{2,0,1:T(2,128)} %copy.179), calls=%async_computation.1 | async-start | bytes 262144 | tf_op jit(solution)/shard_map/all_to_all | solution.py:159
Sparse Core Ops, SparseCore 0:
  82.1 79.6 all-gather.2
  220.5 208.0 all-gather.4
  617.2 185.2 all-reduce.2
where the time goes:
time: 832 us; the launch traced here: 828 us
  blocking collectives  432 us (52%)
  waiting for transfers between devices  196 us (24%)
  other arithmetic  65.2 us (8%)
  local copies, waits for them, and re-layouts  52 us (6%)
  loops' own time  43.2 us (5%)
  starting transfers between devices  16.1 us (2%)
  between operations  14.8 us (2%)
  matrix products  8.74 us (1%)
    psum x1, blocking collectives, local(): weight_sum, gain_sum = lax.psum((weight_part, gain_part), 'seq')  252 us
    psum x1, waiting for transfers between devices, local(): weight_sum, gain_sum = lax.psum((weight_part, gain_part), 'seq')  184 us
    unnamed x1, blocking collectives  126 us
    select_n x63, other arithmetic, chain_states(): jnp.where(late_flag > 0.0, late_state, early_state + late_state)  54.7 us
    all_gather x1, blocking collectives, local(): rows_full = lax.all_gather(feature_weight, 'seq', axis=2, tiled=True)  53.9 us
    another operation x2, loops' own time, carried_in(): return lax.fori_loop(0, ahead, one, state)  43.2 us
    dynamic_slice x63, local copies, waits for them, and re-layouts, one(): lax.dynamic_index_in_dim(a, source, 0, False).astype(own.dtype)  37 us
  transfers between devices with their start and end apart: 5, of which 3 were waited for; matrix products, arithmetic and copies ran while one was open for 2% of the time, Pallas kernels for 0%

commit v1 on v0

--- a/solution.py
+++ b/solution.py
@@ -47,7 +47,9 @@
 
 
 def local(queries, keys, values, feature_weight, norm_gain, doc_bounds, out_grad):
-    rows_full = lax.all_gather(feature_weight, "seq", axis=2, tiled=True)
+    rows_full = jnp.concatenate(
+        lax.all_to_all(jnp.stack([feature_weight] * lax.axis_size("seq")), "seq", 0, 0), axis=2
+    )
     weight_local = lax.all_to_all(rows_full, "fsdp", split_axis=0, concat_axis=1, tiled=True)
     head_count = weight_local.shape[0]
     tokens_here = queries.shape[0]

time: 832 us -> 801 us (0.963)
  blocking collectives: 432 us -> 377 us
  starting transfers between devices: 16.1 us -> 28.9 us
  waiting for transfers between devices: 196 us -> 205 us
    all_gather x1 -> x0, blocking collectives: 53.9 us -> none  [local(): rows_full = lax.all_gather(feature_weight, 'seq', axis=2, tiled=True)]
    all_to_all x0 -> x1, starting transfers between devices: none -> 11.6 us  [local(): lax.all_to_all(jnp.stack([feature_weight] * lax.axis_size('seq')), 'seq',...]
    all_to_all x0 -> x1, waiting for transfers between devices: none -> 9.4 us  [local(): lax.all_to_all(jnp.stack([feature_weight] * lax.axis_size('seq')), 'seq',...]
  transfers between devices with their start and end apart: 5 -> 6, of which waited for: 3 -> 4; matrix products, arithmetic and copies ran while one was open for 2% -> 2% of each run, Pallas kernels for 0% -> 0%
where the time goes in v1:
time: 801 us; the launch traced here: 796 us
  blocking collectives  377 us (47%)
  waiting for transfers between devices  205 us (26%)
  other arithmetic  65.4 us (8%)
  local copies, waits for them, and re-layouts  53.5 us (7%)
  loops' own time  43.1 us (5%)
  starting transfers between devices  28.9 us (4%)
  between operations  14.8 us (2%)
  matrix products  8.74 us (1%)
    psum x1, blocking collectives, local(): weight_sum, gain_sum = lax.psum((weight_part, gain_part), 'seq')  252 us
    psum x1, waiting for transfers between devices, local(): weight_sum, gain_sum = lax.psum((weight_part, gain_part), 'seq')  183 us
    unnamed x1, blocking collectives  126 us
    select_n x63, other arithmetic, chain_states(): jnp.where(late_flag > 0.0, late_state, early_state + late_state)  54.7 us
    another operation x2, loops' own time, carried_in(): return lax.fori_loop(0, ahead, one, state)  43.1 us
    dynamic_slice x63, local copies, waits for them, and re-layouts, one(): lax.dynamic_index_in_dim(a, source, 0, False).astype(own.dtype)  37 us
  transfers between devices with their start and end apart: 6, of which 4 were waited for; matrix products, arithmetic and copies ran while one was open for 2% of the time, Pallas kernels for 0%

profile of v1, /device:TPU:1, one launch (start us, length us, event | category | flops | bytes accessed | tf_op | source)
XLA Modules:
  0.0 796.4 jit_solution(11939907995261651431)
XLA Ops:
  8.0 1.1 reshape.131
  9.1 11.6 %all-to-all-start = ((bf16[64,2,256]{2,1,0:T(2,128)(2,1)}), bf16[64,2,256]{2,1,0:T(2,128)(2,1)S(1)}, u32[]{:S(2)}, u32[]{:S(2)}) async-start(bf16[64,2,256]{2,1,0:T(2,128)(2,1)} %reshape.131), calls=%async_computation | async-start | bytes 131072 | tf_op jit(solution)/shard_map/all_to_all | solution.py:51
  21.4 9.4 %all-to-all-done = bf16[64,2,256]{2,1,0:T(2,128)(2,1)S(1)} async-done(((bf16[64,2,256]{2,1,0:T(2,128)(2,1)}), bf16[64,2,256]{2,1,0:T(2,128)(2,1)S(1)}, u32[]{:S(2)}, u32[]{:S(2)}) %all-to-all-start) | async-done | bytes 65568 | tf_op jit(solution)/shard_map/all_to_all | solution.py:51
  31.2 1.1 copy.116
  32.3 10.0 %all-to-all-start.1 = ((bf16[16,16,128]{2,1,0:T(8,128)(2,1)}), bf16[16,16,128]{2,1,0:T(8,128)(2,1)S(1)}, u32[]{:S(2)}, u32[]{:S(2)}) async-start(bf16[16,16,128]{2,1,0:T(8,128)(2,1)} %copy.116), calls=%async_computation.1 | async-start | bytes 131072 | tf_op jit(solution)/shard_map/all_to_all | solution.py:53
  43.0 1.0 reshape.110
  44.1 1.0 reshape.111
  45.7 3.8 all-to-all-done.1
  50.0 2.6 fusion.43
  54.7 1.3 dynamic-slice
  56.7 125.7 %all-reduce = bf16[64]{0:T(256)(128)(2,1)S(1)} all-reduce(bf16[64]{0:T(256)(128)(2,1)S(1)} %dynamic-update-slice), channel_id=1, replica_groups=mesh['seq'=64,'fsdp'=8] {'seq'}, use_global_device_ids=true, to_apply=%add | all-reduce | flops 64 | bytes 256
  184.6 2.1 while.26
  187.9 3.3 fusion.40
  191.6 1.2 fusion.48
  193.7 0.9 copy.129
  194.6 251.6 %psum.15 = f32[2,128]{1,0:T(2,128)S(1)} all-reduce(f32[2,128]{1,0:T(2,128)S(1)} %get-tuple-element.136), channel_id=1, replica_groups=mesh['seq'=64,'fsdp'=8] {'seq'}, use_global_device_ids=true, to_apply=%region_11.12 | all-reduce | flops 256 | bytes 2048 | tf_op jit(solution)/shard_map/psum | solution.py:156
  446.8 1.5 fusion.41
  448.4 1.9 copy_bitcast_fusion.2
  450.2 132.8 %while.27 = (s32[]{:T(128)}, f32[2,128,128]{2,1,0:T(8,128)S(1)}, s32[]{:T(128)}, bf16[64]{0:T(256)(128)(2,1)S(1)}, bf16[64,2,128,128]{3,2,1,0:T(8,128)(2,1)}, /*...) while((s32[]{:T(128)}, f32[2,128,128]{2,1,0:T(8,128)S(1)}, s32[]{:T(128)}, ...), condition=%wide.region_8.9_spmd, body=%wide.region_7.8_spmd.sunk | while | flops 98311 | bytes 327847 | solution.py:31
  583.0 1.4 fusion.29
  584.4 1.4 fusion.34
  588.1 182.9 %all-reduce.3.cloned.1.call-done = f32[2,128,128]{1,2,0:T(8,128)} async-done(((f32[2,128,128]{1,2,0:T(8,128)}), f32[2,128,128]{1,2,0:T(8,128)}) %all-reduce.3.cloned.1.call-update) | async-done | bytes 131088 | tf_op jit(solution)/shard_map/psum | solution.py:156
  772.6 7.1 all-to-all-start.2
  780.5 8.5 %all-to-all-done.2 = f32[2,128,2]{2,0,1:T(2,128)S(1)} async-done(((f32[2,128,2]{2,0,1:T(2,128)}), f32[2,128,2]{2,0,1:T(2,128)S(1)}, u32[]{:S(2)}, u32[]{:S(2)}) %all-to-all-start.2) | async-done | bytes 2080 | tf_op jit(solution)/shard_map/all_to_all | solution.py:161
  (201 shorter events, 108.2 us)
Async XLA Ops:
  7.2 46.2 %copy-start.2 = (bf16[512,256]{1,0:T(8,128)(2,1)S(1)}, bf16[512,256]{1,0:T(8,128)(2,1)}, u32[]{:S(2)}) copy-start(bf16[512,256]{1,0:T(8,128)(2,1)} %param.11) | copy-start | bytes 786436
  7.2 47.0 %copy-start.1 = (bf16[512,256]{1,0:T(8,128)(2,1)S(1)}, bf16[512,256]{1,0:T(8,128)(2,1)}, u32[]{:S(2)}) copy-start(bf16[512,256]{1,0:T(8,128)(2,1)} %param.17) | copy-start | bytes 786436
  8.0 46.7 %copy-start.7 = (bf16[2,128]{1,0:T(2,128)(2,1)S(1)}, bf16[2,128]{1,0:T(2,128)(2,1)}, u32[]{:S(2)}) copy-start(bf16[2,128]{1,0:T(2,128)(2,1)} %param.15) | copy-start | bytes 1540
  9.1 21.7 %all-to-all-start = ((bf16[64,2,256]{2,1,0:T(2,128)(2,1)}), bf16[64,2,256]{2,1,0:T(2,128)(2,1)S(1)}, u32[]{:S(2)}, u32[]{:S(2)}) async-start(bf16[64,2,256]{2,1,0:T(2,128)(2,1)} %reshape.131), calls=%async_computation | async-start | bytes 131072 | tf_op jit(solution)/shard_map/all_to_all | solution.py:51
  32.3 17.3 %all-to-all-start.1 = ((bf16[16,16,128]{2,1,0:T(8,128)(2,1)}), bf16[16,16,128]{2,1,0:T(8,128)(2,1)S(1)}, u32[]{:S(2)}, u32[]{:S(2)}) async-start(bf16[16,16,128]{2,1,0:T(8,128)(2,1)} %copy.116), calls=%async_computation.1 | async-start | bytes 131072 | tf_op jit(solution)/shard_map/all_to_all | solution.py:53
  42.3 142.3 %all-gather.3.cloned.1.call-start = ((), (), s32[]{:S(2)}) async-start(), calls=%async_computation.3 | async-start | bytes 4259840 | tf_op jit(solution)/shard_map/all_gather | solution.py:16
  52.6 397.6 %all-gather.5.cloned.1.call-start = ((), (), s32[]{:S(2)}) async-start(), calls=%async_computation.4 | async-start | bytes 4259840 | tf_op jit(solution)/shard_map/all_gather | solution.py:16
  54.5 132.3 %copy-start.6 = (f32[1,2,128,128]{3,2,1,0:T(8,128)S(1)}, f32[1,2,128,128]{3,2,1,0:T(8,128)}, u32[]{:S(2)}) copy-start(f32[1,2,128,128]{3,2,1,0:T(8,128)} %get-tuple-element.165) | copy-start | bytes 393220
  183.7 3.7 copy-start.4
  186.8 6.4 copy-start.3
  191.2 579.8 %all-reduce.3.cloned.1.call-start = ((), (), s32[]{:S(2)}) async-start(), calls=%async_computation.5 | async-start | bytes 262144 | tf_op jit(solution)/shard_map/psum | solution.py:156
  194.6 389.8 %copy-start = (f32[1,2,128,128]{3,2,1,0:T(8,128)S(1)}, f32[1,2,128,128]{3,2,1,0:T(8,128)}, u32[]{:S(2)}) copy-start(f32[1,2,128,128]{3,2,1,0:T(8,128)} %get-tuple-element.161) | copy-start | bytes 393220
  448.4 134.7 %copy-start.5 = (f32[1,2,128,128]{3,2,1,0:T(8,128)}, f32[1,2,128,128]{3,2,1,0:T(8,128)S(1)}, u32[]{:S(2)}) copy-start(f32[1,2,128,128]{3,2,1,0:T(8,128)S(1)} %fusion.41) | copy-start | bytes 393220
  772.6 16.4 %all-to-all-start.2 = ((f32[2,128,2]{2,0,1:T(2,128)}), f32[2,128,2]{2,0,1:T(2,128)S(1)}, u32[]{:S(2)}, u32[]{:S(2)}) async-start(f32[2,128,2]{2,0,1:T(2,128)} %copy.148), calls=%async_computation.2 | async-start | bytes 262144 | tf_op jit(solution)/shard_map/all_to_all | solution.py:161
Sparse Core Ops, SparseCore 0:
  52.8 75.5 all-gather.2
  191.3 205.3 all-gather.4
  587.3 183.7 all-reduce.2
